TPU v7x, 256 devices: a whole 4x4x8 slice. The times are simulated.
256 devices in a mesh: space: 16 (over x_hi, z), chan: 8 (over y, core), dp: 2 (over x_lo).
Axes of the slice: x: 4 (x_hi: 2, x_lo: 2; x = x_hi * 2 + x_lo), y: 4, z: 8, core: 2. Of those that a mesh axis runs over, the one named last changes fastest.
Arguments:
- inputs: bfloat16 [2, 32, 8, 128, 512], P('dp', 'space', None, 'chan'), may hold values from -6 to 6
- cotangent: bfloat16 [2, 32, 8, 128, 512], P('dp', 'space', None, 'chan'), may hold values from -6 to 6
- weight: bfloat16 [27, 128, 128], P(None, 'chan'), may hold values from -0.109375 to 0.109375
Outputs:
- input_grad: bfloat16 [2, 32, 8, 128, 512], P('dp', 'space', None, 'chan')
- weight_grad: float32 [27, 128, 128], P(None, 'chan')
All inputs are finite; a program needn't handle non-finite values.
Results may differ from a plain program's by a relative error of at most 0.001.
Values may be sent and summed in bfloat16 or wider, within the bound.
No kernel may reach another device: no remote copies, remote signals or barrier semaphores. Data moves between devices by JAX's collectives and lax.ppermute only.
A program may use at most 64 MiB of HBM per device.

v0:
```python
import math
import jax
import jax.numpy as jnp
from jax import lax
from jax.sharding import PartitionSpec as P


def from_behind(value, axis, steps):
    count = lax.axis_size(axis)
    initial, last = (max(0, -steps), min(count, count - steps))
    return lax.ppermute(value, axis, [(source, source + steps) for source in range(initial, last)])


def shift_cells(block, step_z, step_y):
    zero = jnp.zeros((), block.dtype)
    config = ((0, 0, 0), (0, 0, 0), (step_z, -step_z, 0), (0, 0, 0), (step_y, -step_y, 0))
    return lax.pad(block, zero, config)


def local(inputs, cotangent, weight):
    samples, planes, depth, channels, width = inputs.shape
    outputs = weight.shape[2]
    gathered = lax.all_gather(cotangent, "chan", axis=3, tiled=True)
    lower_plane = from_behind(gathered[:, -1:], "space", 1)
    upper_plane = from_behind(gathered[:, :1], "space", -1)
    stacked = jnp.concatenate(
        [shift_cells(inputs, -step_z, -step_y) for step_z in (-1, 0, 1) for step_y in (-1, 0, 1)],
        axis=3,
    )
    accum = jnp.zeros(inputs.shape, jnp.float32)
    groups = []
    for step_x in (-1, 0, 1):
        if step_x == 1:
            slab = jnp.concatenate([lower_plane, gathered[:, : planes - 1]], axis=1)
        elif step_x == -1:
            slab = jnp.concatenate([gathered[:, 1:], upper_plane], axis=1)
        else:
            slab = gathered
        first = 9 * (step_x + 1)
        groups.append(
            jnp.einsum("bxzky,bxzcy->kc", stacked, slab, preferred_element_type=jnp.float32)
        )
        for step_y in (-1, 0, 1):
            kernel = weight[first + step_y + 1 : first + 9 : 3].reshape(3 * channels, outputs)
            product = jnp.einsum(
                "bxzcy,kc->bxzky", slab, kernel, preferred_element_type=jnp.float32
            )
            for place, step_z in enumerate((-1, 0, 1)):
                part = product[:, :, :, place * channels : (place + 1) * channels]
                accum = accum + shift_cells(part, step_z, step_y)
    input_grad = accum.astype(jnp.bfloat16)
    local_grad = jnp.concatenate(groups, axis=0).reshape(27, channels, outputs)
    count = samples * lax.axis_size("dp") * planes * lax.axis_size("space") * depth * width
    scale = 1.0 / math.sqrt(count)
    weight_grad = lax.psum(local_grad, ("space", "dp")) * scale
    return (input_grad, weight_grad)


def solution(mesh):
    placed = (
        P("dp", "space", None, "chan", None),
        P("dp", "space", None, "chan", None),
        P(None, "chan", None),
    )
    return jax.shard_map(
        local,
        mesh=mesh,
        in_specs=placed,
        out_specs=(P("dp", "space", None, "chan", None), P(None, "chan", None)),
        check_vma=False,
    )
```

profile of v0, /device:TPU:2, one launch (start us, length us, event | category | flops | bytes accessed | tf_op | source)
XLA Modules:
  0.0 232.0 jit_solution(5952417123900889191)
XLA Ops:
  7.2 0.7 all-gather.2.cloned.1.call-update
  8.0 1.1 fusion.64
  9.0 1.0 fusion.60
  10.0 1.1 fusion.65
  11.1 1.1 fusion.62
  12.7 1.4 copy-done.5
  14.2 26.5 %all-gather.2.cloned.1.call-done = bf16[1,2,8,128,512]{4,3,2,1,0:T(8,128)(2,1)} async-done(((bf16[1,2,8,16,512]{4,3,2,1,0:T(8,128)(2,1)}), bf16[1,2,8,128,512]{4,3,2,1,0:T(8,128)(2,1)}) %all-gather.2.cloned.1.call-update) | async-done | bytes 2097168 | tf_op jit(solution)/shard_map/all_gather | solution.py:23
  40.7 1.9 fusion.68
  42.6 3.5 %collective-permute-start.1 = (bf16[1,1,8,128,512]{4,3,2,1,0:T(8,128)(2,1)S(1)}, bf16[1,1,8,128,512]{4,3,2,1,0:T(8,128)(2,1)S(1)}, u32[]{:S(2)}, u32[]{:S(2)}) collective-permute-start(bf16[1,1,8,128,512]{4,3,2,1,0:T(8,128)(2,1)S(1)} %get-tuple-element.2), channel_id=1, source_target_pairs={{0,16},{16,32},{32,48},{48,64},{64,80},{80,96},{96,112},{112,128},... | collective-permute-start | bytes 3145736 | tf_op jit(solution)/shard_map/ppermute | solution.py:11
  46.1 1.3 collective-permute-start
  47.4 0.4 fusion.16
  47.9 0.4 fusion.19
  48.3 0.4 fusion.13
  48.7 0.3 copy-done.4
  49.0 1.5 fusion.72
  50.5 1.2 fusion.74
  51.7 1.1 copy-done.6
  52.8 0.8 fusion.25
  53.5 19.5 %collective-permute-done = bf16[1,1,8,128,512]{4,3,2,1,0:T(8,128)(2,1)S(1)} collective-permute-done((bf16[1,1,8,128,512]{4,3,2,1,0:T(8,128)(2,1)S(1)}, bf16[1,1,8,128,512]{4,3,2,1,0:T(8,128)(2,1)S(1)}, u32[]{:S(2)}, u32[]{:S(2)}) %collective-permute-start) | collective-permute-done | bytes 1048608 | tf_op jit(solution)/shard_map/ppermute | solution.py:11
  73.0 0.4 convolution_bitcast_fusion.3
  73.4 1.2 fusion.71
  74.6 0.4 convolution_bitcast_fusion
  75.1 1.2 fusion.77
  76.3 0.8 fusion.30
  77.1 0.8 fusion.22
  77.8 0.7 pad_maximum_fusion
  78.6 1.7 convolution_bitcast_fusion.4
  80.3 0.4 convolution_bitcast_fusion.5
  80.8 0.4 fusion.69
  81.1 0.4 convolution_bitcast_fusion.1
  81.6 0.4 convolution_bitcast_fusion.2
  82.1 0.4 fusion.75
  82.6 0.2 copy-done.18
  82.7 0.2 copy-done.19
  82.9 0.2 copy-done.20
  83.1 0.3 copy-done.7
  83.3 0.2 copy-done.8
  83.5 0.2 copy-done.9
  83.6 0.2 copy-done.10
  83.8 0.2 copy-done.11
  84.0 0.2 copy-done.12
  84.1 0.2 copy-done.13
  84.3 0.2 copy-done.14
  84.4 0.2 copy-done.15
  84.6 0.2 copy-done.16
  84.7 4.3 %fusion.59 = bf16[1,2,8,16,512]{4,3,2,1,0:T(8,128)(2,1)} fusion(f32[1,2,8,16,512]{4,3,2,1,0:T(8,128)S(1)} %copy-done.19, f32[1,2,8,16,512]{4,3,2,1,0:T(8,128)S(1)} %copy-done.20, f32[1,2,8,16,512]{4,3,2,1,0:T(8,128)S(1)} %copy-done.18, f32[1,2,8,16,512]{4,3,2,1,0:T(8,128)S(1)} %get-tuple-element.41, f32[1,2,8,48,512]{4,3,2,1,0:T(8,128)S(1)} %convolution_bitcast_fusion.1, ...), kind=kLoop, calls=%fused_computation.77 | loop fusion | flops 3538944 | bytes 14417920 | tf_op jit(solution)/shard_map/convert_element_type | solution.py:51
  89.0 134.5 %all-reduce.34.cloned.1.call-done = f32[27,16,128]{2,1,0:T(8,128)} async-done(((f32[27,16,128]{2,1,0:T(8,128)}), f32[27,16,128]{2,1,0:T(8,128)}) %all-reduce.34.cloned.1.call-update) | async-done | bytes 221200 | tf_op jit(solution)/shard_map/psum | solution.py:55
  223.5 1.6 broadcast_multiply_fusion
  (38 shorter events, 0.7 us)
Async XLA Ops:
  7.2 5.1 %copy-start.1 = (bf16[1,2,8,16,512]{4,3,2,1,0:T(8,128)(2,1)S(1)}, bf16[1,2,8,16,512]{4,3,2,1,0:T(8,128)(2,1)}, u32[]{:S(2)}) copy-start(bf16[1,2,8,16,512]{4,3,2,1,0:T(8,128)(2,1)} %param.3) | copy-start | bytes 786436
  7.2 33.5 %all-gather.2.cloned.1.call-start = ((), (), s32[]{:S(2)}) async-start(), calls=%async_computation | async-start | bytes 2359296 | tf_op jit(solution)/shard_map/all_gather | solution.py:23
  7.9 215.6 %all-reduce.34.cloned.1.call-start = ((), (), s32[]{:S(2)}) async-start(), calls=%async_computation.1 | async-start | bytes 442368 | tf_op jit(solution)/shard_map/psum | solution.py:55
  9.0 5.1 %copy-start.21 = (bf16[27,16,128]{2,1,0:T(8,128)(2,1)S(1)}, bf16[27,16,128]{2,1,0:T(8,128)(2,1)}, u32[]{:S(2)}) copy-start(bf16[27,16,128]{2,1,0:T(8,128)(2,1)} %param.5) | copy-start | bytes 331780
  12.7 1.4 copy-start.5
  40.7 6.7 %copy-start = (bf16[1,2,8,128,512]{4,3,2,1,0:T(8,128)(2,1)S(1)}, bf16[1,2,8,128,512]{4,3,2,1,0:T(8,128)(2,1)}, u32[]{:S(2)}) copy-start(bf16[1,2,8,128,512]{4,3,2,1,0:T(8,128)(2,1)} %all-gather.2.cloned.1.call-done) | copy-start | bytes 6291460
  42.6 32.1 %collective-permute-start.1 = (bf16[1,1,8,128,512]{4,3,2,1,0:T(8,128)(2,1)S(1)}, bf16[1,1,8,128,512]{4,3,2,1,0:T(8,128)(2,1)S(1)}, u32[]{:S(2)}, u32[]{:S(2)}) collective-permute-start(bf16[1,1,8,128,512]{4,3,2,1,0:T(8,128)(2,1)S(1)} %get-tuple-element.2), channel_id=1, source_target_pairs={{0,16},{16,32},{32,48},{48,64},{64,80},{80,96},{96,112},{112,128},... | collective-permute-start | bytes 3145736 | tf_op jit(solution)/shard_map/ppermute | solution.py:11
  46.1 26.9 %collective-permute-start = (bf16[1,1,8,128,512]{4,3,2,1,0:T(8,128)(2,1)S(1)}, bf16[1,1,8,128,512]{4,3,2,1,0:T(8,128)(2,1)S(1)}, u32[]{:S(2)}, u32[]{:S(2)}) collective-permute-start(bf16[1,1,8,128,512]{4,3,2,1,0:T(8,128)(2,1)S(1)} %get-tuple-element.3), channel_id=1, source_target_pairs={{16,0},{32,16},{48,32},{64,48},{80,64},{96,80},{112,96},{128,112},... | collective-permute-start | bytes 3145736 | tf_op jit(solution)/shard_map/ppermute | solution.py:11
  47.8 1.2 copy-start.4
  50.5 2.2 copy-start.6
  73.0 4.0 %copy-start.2 = (bf16[1,1,8,128,512]{4,3,2,1,0:T(8,128)(2,1)}, bf16[1,1,8,128,512]{4,3,2,1,0:T(8,128)(2,1)S(1)}, u32[]{:S(2)}) copy-start(bf16[1,1,8,128,512]{4,3,2,1,0:T(8,128)(2,1)S(1)} %collective-permute-done) | copy-start | bytes 3145732
  78.6 1.7 copy-start.3
  81.5 1.0 copy-start.17
  81.5 1.2 copy-start.18
  81.6 1.3 copy-start.19
  81.6 1.5 copy-start.20
  82.0 1.3 copy-start.7
  82.0 1.5 copy-start.8
  82.0 1.6 copy-start.9
  82.0 1.8 copy-start.10
  82.0 1.9 copy-start.11
  82.0 2.1 copy-start.12
  82.1 2.2 copy-start.13
  82.1 2.4 %copy-start.14 = (f32[1,2,8,16,512]{4,3,2,1,0:T(8,128)S(1)}, f32[1,2,8,16,512]{4,3,2,1,0:T(8,128)}, u32[]{:S(2)}) copy-start(f32[1,2,8,16,512]{4,3,2,1,0:T(8,128)} %get-tuple-element.19) | copy-start | bytes 1572868
  82.1 2.5 %copy-start.15 = (f32[1,2,8,16,512]{4,3,2,1,0:T(8,128)S(1)}, f32[1,2,8,16,512]{4,3,2,1,0:T(8,128)}, u32[]{:S(2)}) copy-start(f32[1,2,8,16,512]{4,3,2,1,0:T(8,128)} %get-tuple-element.9) | copy-start | bytes 1572868
  82.1 2.7 %copy-start.16 = (f32[1,2,8,16,512]{4,3,2,1,0:T(8,128)S(1)}, f32[1,2,8,16,512]{4,3,2,1,0:T(8,128)}, u32[]{:S(2)}) copy-start(f32[1,2,8,16,512]{4,3,2,1,0:T(8,128)} %get-tuple-element.10) | copy-start | bytes 1572868
Sparse Core Ops, SparseCore 0:
  9.8 30.8 all-gather.1
  78.7 144.8 all-reduce.33
where the time goes:
time: 232 us
  waiting for transfers between devices  181 us (78%)
  local copies, waits for them, and re-layouts  17.5 us (8%)
  between operations  14.4 us (6%)
  matrix products  7.41 us (3%)
  other arithmetic  6.63 us (3%)
  starting transfers between devices  4.89 us (2%)
    psum x1, waiting for transfers between devices, local(): weight_grad = lax.psum(local_grad, ('space', 'dp')) * scale  134 us
    all_gather x1, waiting for transfers between devices, local(): gathered = lax.all_gather(cotangent, 'chan', axis=3, tiled=True)  26.5 us
    ppermute x2, waiting for transfers between devices, from_behind(): lax.ppermute(value, axis, [(source, source + steps) for source in range(i...  19.5 us
    unnamed x52, local copies, waits for them, and re-layouts  9.68 us
    slice x6, local copies, waits for them, and re-layouts, local(): part = product[:, :, :, place * channels:(place + 1) * channels]  5.81 us
    dot_general x9, matrix products, local(): jnp.einsum('bxzcy,kc->bxzky', slab, kernel, preferred_element_type=jnp.fl...  5.09 us
    ppermute x2, starting transfers between devices, from_behind(): lax.ppermute(value, axis, [(source, source + steps) for source in range(i...  4.82 us
  transfers between devices with their start and end apart: 4, of which 3 were waited for; matrix products, arithmetic and copies ran while one was open for 8% of the time, Pallas kernels for 0%

commit v1 on v0

--- a/solution.py
+++ b/solution.py
@@ -52,7 +52,7 @@
     local_grad = jnp.concatenate(groups, axis=0).reshape(27, channels, outputs)
     count = samples * lax.axis_size("dp") * planes * lax.axis_size("space") * depth * width
     scale = 1.0 / math.sqrt(count)
-    weight_grad = lax.psum(local_grad, ("space", "dp")) * scale
+    weight_grad = jnp.sum(lax.all_gather(local_grad, ("space", "dp")), axis=0) * scale
     return (input_grad, weight_grad)
 
 

time: 232 us -> 256 us (1.10)
  waiting for transfers between devices: 181 us -> 201 us
  matrix products: 7.41 us -> 11.9 us
  local copies, waits for them, and re-layouts: 17.5 us -> 13.8 us
    all_gather x0 -> x1, waiting for transfers between devices: none -> 155 us  [local(): lax.all_gather(local_grad, ('space', 'dp'))]
    psum x1 -> x0, waiting for transfers between devices: 134 us -> none  [local(): weight_grad = lax.psum(local_grad, ('space', 'dp')) * scale]
    dot_general x3, matrix products: 2.31 us -> 8.07 us  [local(): jnp.einsum('bxzky,bxzcy->kc', stacked, slab, preferred_element_type=jnp.f...]
    slice x6, local copies, waits for them, and re-layouts: 5.81 us -> 1.65 us  [local(): part = product[:, :, :, place * channels:(place + 1) * channels]]
    reduce_sum x0 -> x1, other arithmetic: none -> 3.46 us  [local(): jnp.sum(lax.all_gather(local_grad, ('space', 'dp')), axis=0) * scale]
    all_gather x1, waiting for transfers between devices: 26.5 us -> 29.3 us  [local(): gathered = lax.all_gather(cotangent, 'chan', axis=3, tiled=True)]
    unnamed x52 -> x26, local copies, waits for them, and re-layouts: 9.68 us -> 9.59 us
  transfers between devices with their start and end apart: 4 -> 4, of which waited for: 3 -> 4; matrix products, arithmetic and copies ran while one was open for 8% -> 9% of each run, Pallas kernels for 0% -> 0%
where the time goes in v1:
time: 256 us; the launch traced here: 255 us
  waiting for transfers between devices  201 us (79%)
  between operations  14.2 us (6%)
  local copies, waits for them, and re-layouts  13.8 us (5%)
  matrix products  11.9 us (5%)
  other arithmetic  8.25 us (3%)
  starting transfers between devices  5.14 us (2%)
    all_gather x1, waiting for transfers between devices, local(): lax.all_gather(local_grad, ('space', 'dp'))  155 us
    all_gather x1, waiting for transfers between devices, local(): gathered = lax.all_gather(cotangent, 'chan', axis=3, tiled=True)  29.3 us
    ppermute x2, waiting for transfers between devices, from_behind(): lax.ppermute(value, axis, [(source, source + steps) for source in range(i...  17 us
    unnamed x26, local copies, waits for them, and re-layouts  9.59 us
    dot_general x3, matrix products, local(): jnp.einsum('bxzky,bxzcy->kc', stacked, slab, preferred_element_type=jnp.f...  8.07 us
  transfers between devices with their start and end apart: 4, of which 4 were waited for; matrix products, arithmetic and copies ran while one was open for 9% of the time, Pallas kernels for 0%

profile of v1, /device:TPU:2, one launch (start us, length us, event | category | flops | bytes accessed | tf_op | source)
XLA Modules:
  0.0 254.8 jit_solution(3066578206456327360)
XLA Ops:
  7.2 0.0 all-gather.3.cloned.1.call-start
  7.2 0.7 all-gather.3.cloned.1.call-update
  7.9 0.0 all-gather.5.cloned.1.call-start
  7.9 1.8 fusion.64
  9.7 1.7 fusion.60
  11.4 29.3 %all-gather.3.cloned.1.call-done = bf16[1,2,8,128,512]{4,3,2,1,0:T(8,128)(2,1)} async-done(((bf16[1,2,8,16,512]{4,3,2,1,0:T(8,128)(2,1)}), bf16[1,2,8,128,512]{4,3,2,1,0:T(8,128)(2,1)}) %all-gather.3.cloned.1.call-update) | async-done | bytes 2097168 | tf_op jit(solution)/shard_map/all_gather | solution.py:23
  40.7 1.7 fusion.68
  42.4 3.8 %collective-permute-start.1 = (bf16[1,1,8,128,512]{4,3,2,1,0:T(8,128)(2,1)S(1)}, bf16[1,1,8,128,512]{4,3,2,1,0:T(8,128)(2,1)S(1)}, u32[]{:S(2)}, u32[]{:S(2)}) collective-permute-start(bf16[1,1,8,128,512]{4,3,2,1,0:T(8,128)(2,1)S(1)} %get-tuple-element.2), channel_id=1, source_target_pairs={{0,16},{16,32},{32,48},{48,64},{64,80},{80,96},{96,112},{112,128},... | collective-permute-start | bytes 3145736 | tf_op jit(solution)/shard_map/ppermute | solution.py:11
  46.2 0.9 fusion.65
  47.2 0.8 fusion.62
  48.0 0.7 constant_dynamic-update-slice_fusion
  48.7 1.3 collective-permute-start
  50.0 0.9 fusion.63
  50.9 0.8 fusion.66
  51.7 0.7 fusion.61
  52.5 0.9 fusion.67
  53.3 2.4 fusion.25
  55.8 13.2 %collective-permute-done.1 = bf16[1,1,8,128,512]{4,3,2,1,0:T(8,128)(2,1)S(1)} collective-permute-done((bf16[1,1,8,128,512]{4,3,2,1,0:T(8,128)(2,1)S(1)}, bf16[1,1,8,128,512]{4,3,2,1,0:T(8,128)(2,1)S(1)}, u32[]{:S(2)}, u32[]{:S(2)}) %collective-permute-start.1) | collective-permute-done | bytes 1048608 | tf_op jit(solution)/shard_map/ppermute | solution.py:11
  69.0 2.8 %fusion.30 = f32[144,128]{1,0:T(8,128)S(1)} fusion(bf16[1,2,8,144,512]{4,3,2,1,0:T(8,128)(2,1)} %fusion.67, bf16[1,1,8,128,512]{4,3,2,1,0:T(8,128)(2,1)S(1)} %get-tuple-element.3, bf16[1,1,8,128,512]{4,3,2,1,0:T(8,128)(2,1)S(1)} %collective-permute-done.1), kind=kOutput, calls=%fused_computation.26 | convolution fusion | flops 303038464 | bytes 4530176 | tf_op jit(solution)/shard_map/bxzky,bxzcy->kc/dot_general | solution.py:41
  71.8 0.0 copy-start.8
  71.8 3.8 %collective-permute-done = bf16[1,1,8,128,512]{4,3,2,1,0:T(8,128)(2,1)S(1)} collective-permute-done((bf16[1,1,8,128,512]{4,3,2,1,0:T(8,128)(2,1)S(1)}, bf16[1,1,8,128,512]{4,3,2,1,0:T(8,128)(2,1)S(1)}, u32[]{:S(2)}, u32[]{:S(2)}) %collective-permute-start) | collective-permute-done | bytes 1048608 | tf_op jit(solution)/shard_map/ppermute | solution.py:11
  75.6 2.8 %fusion.22 = f32[144,128]{1,0:T(8,128)S(1)} fusion(bf16[1,2,8,144,512]{4,3,2,1,0:T(8,128)(2,1)} %fusion.67, bf16[1,1,8,128,512]{4,3,2,1,0:T(8,128)(2,1)S(1)} %collective-permute-done, bf16[1,1,8,128,512]{4,3,2,1,0:T(8,128)(2,1)S(1)} %get-tuple-element.2), kind=kOutput, calls=%fused_computation.24 | convolution fusion | flops 303038464 | bytes 4530176 | tf_op jit(solution)/shard_map/bxzky,bxzcy->kc/dot_general | solution.py:41
  78.5 0.7 pad_maximum_fusion
  79.2 0.0 all-gather.5.cloned.1.call-update
  79.2 0.4 fusion.16
  79.6 0.4 fusion.19
  80.1 0.4 fusion.13
  80.5 0.2 fusion.74
  80.7 0.0 copy-start.3
  80.7 0.0 copy-start.7
  80.7 0.4 fusion.72
  81.1 0.0 copy-start.5
  81.1 0.8 copy-done.3
  81.9 0.3 copy-done.7
  82.2 0.4 convolution_bitcast_fusion.4
  82.6 0.4 convolution_bitcast_fusion.1
  83.1 0.4 convolution_bitcast_fusion.5
  83.5 0.4 convolution_bitcast_fusion.3
  83.9 0.4 convolution_bitcast_fusion.2
  84.3 0.4 convolution_bitcast_fusion
  84.8 0.2 fusion.71
  84.9 0.2 fusion.77
  85.1 0.4 fusion.69
  85.5 0.4 fusion.75
  85.9 3.4 %fusion.59 = bf16[1,2,8,16,512]{4,3,2,1,0:T(8,128)(2,1)} fusion(f32[1,2,8,16,512]{4,3,2,1,0:T(8,128)S(1)} %get-tuple-element.26, f32[1,2,8,16,512]{4,3,2,1,0:T(8,128)S(1)} %get-tuple-element.27, f32[1,2,8,16,512]{4,3,2,1,0:T(8,128)S(1)} %get-tuple-element.25, f32[1,2,8,16,512]{4,3,2,1,0:T(8,128)S(1)} %get-tuple-element.41, ...), kind=kLoop, calls=%fused_computation.77 | loop fusion | flops 3538944 | bytes 14417920 | tf_op jit(solution)/shard_map/convert_element_type | solution.py:51
  89.3 154.5 %all-gather.5.cloned.1.call-done = f32[32,27,16,128]{3,2,1,0:T(8,128)} async-done(((f32[1,27,16,128]{3,2,1,0:T(8,128)}), f32[32,27,16,128]{3,2,1,0:T(8,128)}) %all-gather.5.cloned.1.call-update) | async-done | bytes 7077904 | tf_op jit(solution)/shard_map/all_gather | solution.py:55
  243.8 3.5 %reduce_sum.9 = f32[27,16,128]{2,1,0:T(8,128)S(1)} reduce(f32[32,27,16,128]{3,2,1,0:T(8,128)} %all-gather.5.cloned.1.call-done, f32[]{:T(128)} %constant.0.clone.1), dimensions={0}, to_apply=%region_0.0 | reduce | flops 1714176 | bytes 7299076 | tf_op jit(solution)/shard_map/reduce_sum | solution.py:55
  247.3 0.7 broadcast_multiply_fusion
  (13 shorter events, 0.0 us)
Async XLA Ops:
  7.2 33.5 %all-gather.3.cloned.1.call-start = ((), (), s32[]{:S(2)}) async-start(), calls=%async_computation | async-start | bytes 2359296 | tf_op jit(solution)/shard_map/all_gather | solution.py:23
  7.9 235.9 %all-gather.5.cloned.1.call-start = ((), (), s32[]{:S(2)}) async-start(), calls=%async_computation.1 | async-start | bytes 7299072 | tf_op jit(solution)/shard_map/all_gather | solution.py:55
  11.4 34.8 %copy-start.1 = (bf16[1,2,8,16,512]{4,3,2,1,0:T(8,128)(2,1)S(1)}, bf16[1,2,8,16,512]{4,3,2,1,0:T(8,128)(2,1)}, u32[]{:S(2)}) copy-start(bf16[1,2,8,16,512]{4,3,2,1,0:T(8,128)(2,1)} %param.3) | copy-start | bytes 786436
  42.4 33.2 %copy-start.2 = (bf16[1,1,8,128,512]{4,3,2,1,0:T(8,128)(2,1)}, bf16[1,1,8,128,512]{4,3,2,1,0:T(8,128)(2,1)S(1)}, u32[]{:S(2)}) copy-start(bf16[1,1,8,128,512]{4,3,2,1,0:T(8,128)(2,1)S(1)} %get-tuple-element.2) | copy-start | bytes 3145732
  42.4 10.9 %copy-start = (bf16[1,2,8,128,512]{4,3,2,1,0:T(8,128)(2,1)S(1)}, bf16[1,2,8,128,512]{4,3,2,1,0:T(8,128)(2,1)}, u32[]{:S(2)}) copy-start(bf16[1,2,8,128,512]{4,3,2,1,0:T(8,128)(2,1)} %all-gather.3.cloned.1.call-done) | copy-start | bytes 6291460
  42.4 26.5 %collective-permute-start.1 = (bf16[1,1,8,128,512]{4,3,2,1,0:T(8,128)(2,1)S(1)}, bf16[1,1,8,128,512]{4,3,2,1,0:T(8,128)(2,1)S(1)}, u32[]{:S(2)}, u32[]{:S(2)}) collective-permute-start(bf16[1,1,8,128,512]{4,3,2,1,0:T(8,128)(2,1)S(1)} %get-tuple-element.2), channel_id=1, source_target_pairs={{0,16},{16,32},{32,48},{48,64},{64,80},{80,96},{96,112},{112,128},... | collective-permute-start | bytes 3145736 | tf_op jit(solution)/shard_map/ppermute | solution.py:11
  48.7 26.9 %collective-permute-start = (bf16[1,1,8,128,512]{4,3,2,1,0:T(8,128)(2,1)S(1)}, bf16[1,1,8,128,512]{4,3,2,1,0:T(8,128)(2,1)S(1)}, u32[]{:S(2)}, u32[]{:S(2)}) collective-permute-start(bf16[1,1,8,128,512]{4,3,2,1,0:T(8,128)(2,1)S(1)} %get-tuple-element.3), channel_id=1, source_target_pairs={{16,0},{32,16},{48,32},{64,48},{80,64},{96,80},{112,96},{128,112},... | collective-permute-start | bytes 3145736 | tf_op jit(solution)/shard_map/ppermute | solution.py:11
  69.0 2.8 %copy-start.4 = (bf16[1,1,8,128,512]{4,3,2,1,0:T(8,128)(2,1)}, bf16[1,1,8,128,512]{4,3,2,1,0:T(8,128)(2,1)S(1)}, u32[]{:S(2)}) copy-start(bf16[1,1,8,128,512]{4,3,2,1,0:T(8,128)(2,1)S(1)} %collective-permute-done.1) | copy-start | bytes 3145732
  71.8 7.4 %copy-start.8 = (bf16[27,16,128]{2,1,0:T(8,128)(2,1)S(1)}, bf16[27,16,128]{2,1,0:T(8,128)(2,1)}, u32[]{:S(2)}) copy-start(bf16[27,16,128]{2,1,0:T(8,128)(2,1)} %param.5) | copy-start | bytes 331780
  75.6 2.8 %copy-start.6 = (bf16[1,1,8,128,512]{4,3,2,1,0:T(8,128)(2,1)}, bf16[1,1,8,128,512]{4,3,2,1,0:T(8,128)(2,1)S(1)}, u32[]{:S(2)}) copy-start(bf16[1,1,8,128,512]{4,3,2,1,0:T(8,128)(2,1)S(1)} %collective-permute-done) | copy-start | bytes 3145732
  80.7 1.2 copy-start.3
  80.7 1.5 copy-start.7
  81.1 1.6 copy-start.5
Sparse Core Ops, SparseCore 0:
  9.8 30.8 all-gather.2
  79.3 164.4 all-gather.4
